TPU v7x, 128 devices: a whole 4x4x4 slice. The times are simulated.
128 devices in a mesh: req: 8 (over x, core), seq: 16 (over z, y).
Axes of the slice: x: 4, y: 4, z: 4, core: 2. Of those that a mesh axis runs over, the one named last changes fastest.
Arguments:
- hidden: bfloat16 [8, 2048, 2048], P('req', 'seq'), may hold values from -6 to 6
- lengths: int32 [8], replicated, may hold values from 1 to 2048, 10240 in all
- slot_request: int32 [8], replicated, may hold values from 0 to 7, each once
- norm_gain: bfloat16 [2048], replicated, may hold values from 0.099609375 to 1.8984375
- in_weight: bfloat16 [2, 2048, 4096], P(None, 'req', 'seq'), may hold values from -0.125 to 0.125
- conv_weight: bfloat16 [4, 4096], P(None, 'seq'), may hold values from -3 to 3
- conv_bias: bfloat16 [4096], P('seq'), may hold values from -0.5 to 0.5
- xproj_weight: bfloat16 [4096, 160], P('seq'), may hold values from -0.09375 to 0.09375
- dt_weight: bfloat16 [128, 4096], P(None, 'seq'), may hold values from -0.5 to 0.5
- dt_bias: bfloat16 [4096], P('seq'), may hold values from -6.91 to -2.25
- a_log: float32 [16, 4096], replicated, may hold values from -2.3 to 1.39
- skip_gain: float32 [4096], replicated, may hold values from 0.5 to 1.5
- out_weight: bfloat16 [4096, 2048], P('seq', 'req'), may hold values from -0.09375 to 0.09375
Outputs:
- mixed: bfloat16 [8, 2048, 2048], P('req', 'seq')
- final_state: float32 [8, 16, 4096], P('req', None, 'seq')
Inputs may be any that keep to these rules, and one draw needn't show every extreme that they name: `lengths`: each slot's length is at least 1, the longest is exactly 2048, and they sum to 10240. `slot_request`: A permutation of the requests.
All inputs are finite; a program needn't handle non-finite values.
Results may differ from a plain program's by a relative error of at most 0.015.
Values may be sent and summed in bfloat16 or wider, within the bound.
No kernel may reach another device: no remote copies, remote signals or barrier semaphores. Data moves between devices by JAX's collectives and lax.ppermute only.
A program may use at most 128 MiB of HBM per device.

v0:
```python
import jax
import jax.numpy as jnp
from jax import lax
from jax.sharding import PartitionSpec as P

STATE = 16
RANK = 128


def shifted(block, axis, distance):
    devices = range(lax.axis_size(axis))
    route = [(i - distance, i) for i in devices if i - distance in devices]
    return lax.ppermute(block, axis, route)


def spread(array, axis, root):
    mine = lax.axis_index(axis) == root
    return lax.psum(jnp.where(mine, array, jnp.zeros_like(array)), axis)


def to_blocks(array):
    pieces, length, columns = array.shape
    return jnp.moveaxis(array.reshape(pieces, 16, length // 16, columns), 1, 0)


def from_blocks(array):
    count, pieces, group, columns = array.shape
    return jnp.moveaxis(array, 0, 1).reshape(pieces, count * group, columns)


def piece_scan(rates, values, entry, readout, decay):
    pieces, length, columns = rates.shape
    group = length // 16
    positions = jnp.arange(length, dtype=jnp.int32)
    lower = (positions[None, :] <= positions[:, None]).astype(jnp.float32)
    running = jnp.einsum("rs,psw->prw", lower, rates, precision=lax.Precision.HIGHEST)

    def advance(state, items):
        rate, value, into, outof = items
        outputs = []
        for place in range(group):
            factor = jnp.exp(rate[:, place][:, None, :] * decay[None])
            state = (
                factor * state
                + (rate[:, place] * value[:, place])[:, None, :] * into[:, place][:, :, None]
            )
            outputs.append(jnp.sum(outof[:, place][:, :, None] * state, axis=1))
        return (state, jnp.stack(outputs, axis=1))

    start = jnp.zeros((pieces, decay.shape[0], columns), jnp.float32)
    end_local, local_out = lax.scan(
        advance, start, (to_blocks(rates), to_blocks(values), to_blocks(entry), to_blocks(readout))
    )
    total_decay = jnp.exp(running[:, length - 1][:, None, :] * decay[None])
    return (end_local, from_blocks(local_out), total_decay, running)


def carried_part(running, readout, decay, carry_in):

    def correct(items):
        total, outof = items
        kept = jnp.exp(total[:, :, None, :] * decay[None, None]) * carry_in[:, None]
        return jnp.sum(outof[:, :, :, None] * kept, axis=2)

    return from_blocks(lax.map(correct, (to_blocks(running), to_blocks(readout))))


def per_device(
    hidden,
    lengths,
    slot_request,
    norm_gain,
    in_weight,
    conv_weight,
    conv_bias,
    xproj_weight,
    dt_weight,
    dt_bias,
    a_log,
    skip_gain,
    out_weight,
):
    seq_count = lax.axis_size("seq")
    seq_index = lax.axis_index("seq")
    req_index = lax.axis_index("req")
    rows = hidden.shape[1]
    span = rows * seq_count
    width = in_weight.shape[2]
    taps_count = conv_weight.shape[0]
    state_count = a_log.shape[0]
    total_inner = a_log.shape[1]
    tokens = hidden[0].astype(jnp.float32)
    scale = lax.rsqrt(jnp.mean(tokens * tokens, axis=-1, keepdims=True) + 1e-05)
    normed = (tokens * scale * norm_gain.astype(jnp.float32)).astype(jnp.bfloat16)
    w_in = lax.all_gather(in_weight, "req", axis=1, tiled=True)
    w_flat = jnp.concatenate((w_in[0], w_in[1]), axis=1)
    both = jnp.dot(
        lax.all_gather(normed, "seq", axis=0, tiled=True),
        w_flat,
        preferred_element_type=jnp.float32,
    )
    xin = both[:, :width]
    zgate = both[:, width:].astype(jnp.bfloat16)
    padded = jnp.pad(xin, ((taps_count - 1, 0), (0, 0)))
    taps = conv_weight.astype(jnp.float32)
    convolved = conv_bias.astype(jnp.float32) + jnp.zeros_like(xin)
    for tap in range(taps_count):
        convolved = convolved + taps[tap] * padded[tap : tap + span, :]
    inner = jax.nn.silu(convolved).astype(jnp.bfloat16)
    partial_proj = jnp.dot(inner, xproj_weight, preferred_element_type=jnp.float32)
    length_here = lax.dynamic_index_in_dim(lengths, req_index, 0, keepdims=False)
    summed = lax.psum(partial_proj, "seq")
    live_all = (jnp.arange(span, dtype=jnp.int32) < length_here).astype(jnp.float32)
    rate_low = summed[:, :RANK].astype(jnp.bfloat16)
    delta_ch = (
        jax.nn.softplus(
            jnp.dot(rate_low, dt_weight, preferred_element_type=jnp.float32)
            + dt_bias.astype(jnp.float32)
        )
        * live_all[:, None]
    )
    w_out = lax.all_gather(out_weight, "req", axis=1, tiled=True)
    inner_tok = lax.all_to_all(inner, "seq", split_axis=0, concat_axis=1, tiled=True)
    delta_tok = lax.all_to_all(
        delta_ch.astype(jnp.bfloat16), "seq", split_axis=0, concat_axis=1, tiled=True
    ).astype(delta_ch.dtype)
    own_proj = lax.dynamic_slice_in_dim(summed, seq_index * rows, rows, 0)
    decay = -jnp.exp(a_log)
    inner_f = inner_tok.astype(jnp.float32)
    entry = own_proj[None, :, RANK : RANK + STATE]
    readout = own_proj[None, :, RANK + STATE :]
    end_local, local_out, total_decay, running = piece_scan(
        delta_tok[None], inner_f[None], entry, readout, decay
    )
    zeros_state = jnp.zeros((state_count, total_inner), jnp.float32)

    def relay(turn, incoming):
        return shifted(total_decay[0] * incoming + end_local[0], "seq", 1)

    carry_in = lax.fori_loop(0, seq_count - 1, relay, zeros_state)
    carried = carried_part(running, readout, decay, carry_in[None])
    scanned = ((local_out + carried)[0] + skip_gain * inner_f).astype(jnp.bfloat16)
    last = spread(
        (total_decay[0] * carry_in + end_local[0]).astype(jnp.bfloat16), "seq", seq_count - 1
    ).astype(jnp.float32)
    mine = lax.dynamic_slice_in_dim(last, seq_index * width, width, 1)
    scanned_ch = lax.all_to_all(scanned, "seq", split_axis=1, concat_axis=0, tiled=True)
    gated_ch = (scanned_ch.astype(jnp.float32) * jax.nn.silu(zgate.astype(jnp.float32))).astype(
        jnp.bfloat16
    )
    branch = lax.psum_scatter(
        jnp.dot(gated_ch, w_out, preferred_element_type=jnp.float32).astype(jnp.bfloat16),
        "seq",
        scatter_dimension=0,
        tiled=True,
    ).astype(jnp.float32)
    slot_all = lax.all_gather(mine[None], "req", axis=0, tiled=True)
    picked = (slot_request == req_index).astype(jnp.float32)
    final_state = jnp.sum(picked[:, None, None] * slot_all, axis=0, keepdims=True)
    mixed = (tokens + branch).astype(jnp.bfloat16)[None]
    return (mixed, final_state)


def solution(mesh):
    in_specs = (
        P("req", "seq", None),
        P(),
        P(),
        P(),
        P(None, "req", "seq"),
        P(None, "seq"),
        P("seq"),
        P("seq", None),
        P(None, "seq"),
        P("seq"),
        P(),
        P(),
        P("seq", "req"),
    )
    out_specs = (P("req", "seq", None), P("req", None, "seq"))
    return jax.shard_map(
        per_device, mesh=mesh, in_specs=in_specs, out_specs=out_specs, check_vma=False
    )
```

profile of v0, /device:TPU:0, one launch (start us, length us, event | category | flops | bytes accessed | tf_op | source)
XLA Modules:
  0.0 717.7 jit_solution(14593859675135900258)
XLA Ops:
  12.1 25.4 %all-gather.7.cloned.1.call-done = bf16[2,2048,256]{2,1,0:T(8,128)(2,1)} async-done(((bf16[2,256,256]{2,1,0:T(8,128)(2,1)}), bf16[2,2048,256]{2,1,0:T(8,128)(2,1)}) %all-gather.7.cloned.1.call-update) | async-done | bytes 2097168 | tf_op jit(solution)/shard_map/all_gather | solution.py:95
  39.2 72.3 %all-gather.5.cloned.1.call-done = bf16[2048,2048]{1,0:T(8,128)(2,1)} async-done(((bf16[128,2048]{1,0:T(8,128)(2,1)}), bf16[2048,2048]{1,0:T(8,128)(2,1)}) %all-gather.5.cloned.1.call-update) | async-done | bytes 8388624 | tf_op jit(solution)/shard_map/all_gather | solution.py:98
  111.5 6.9 fusion.33
  125.5 5.4 all-to-all-start.1
  132.2 88.7 %all-reduce.4.cloned.1.call-done = f32[2048,160]{0,1:T(8,128)} async-done(((f32[2048,160]{0,1:T(8,128)}), f32[2048,160]{0,1:T(8,128)}) %all-reduce.4.cloned.1.call-update) | async-done | bytes 1310736 | tf_op jit(solution)/shard_map/psum | solution.py:112
  225.0 5.1 all-to-all-start
  238.4 7.5 %all-to-all-done = bf16[16,128,256]{1,2,0:T(8,128)(2,1)S(1)} async-done(((bf16[16,128,256]{1,2,0:T(8,128)(2,1)}), bf16[16,128,256]{1,2,0:T(8,128)(2,1)S(1)}, u32[]{:S(2)}, u32[]{:S(2)}) %all-to-all-start) | async-done | bytes 1048608 | tf_op jit(solution)/shard_map/all_to_all | solution.py:124
  255.7 65.7 %while.35 = (s32[]{:T(128)}, f32[1,16,4096]{2,1,0:T(8,128)S(1)}, f32[16,1,8,4096]{3,2,1,0:T(8,128)}, f32[16,1,8,4096]{3,2,1,0:T(8,128)}, f32[16,4096]{1,0:T(8,12...) while((s32[]{:T(128)}, f32[1,16,4096]{2,1,0:T(8,128)S(1)}, ...), condition=%wide.region_11.12_spmd.clone, body=%wide.region_2.11_spmd.clone.sunk | while | flops 4849667 | bytes 4347896 | solution.py:51
  321.5 148.6 %while.33 = (s32[]{:T(128)}, f32[16,4096]{1,0:T(8,128)S(1)}, f32[1,16,4096]{2,1,0:T(8,128)S(1)}, f32[1,16,4096]{2,1,0:T(8,128)S(1)}, s32[]{:T(128)}) while((s32[]{:T(128)}, f32[16,4096]{1,0:T(8,128)S(1)}, f32[1,16,4096]{2,1,0:T(8,128)S(1)}, f32[1,16,4096]{2,1,0:T(8,128)S(1)}, s32[]{:T(128)}) %tuple.124), condition=%wide.region_13.14_spmd, body=%wide.region_12.13_spmd.sunk | while | flops 131074 | bytes 2097253 | solution.py:140
  328.0 4.4 collective-permute-start
  332.4 5.0 collective-permute-done
  337.4 4.4 collective-permute-start
  341.8 6.1 collective-permute-done
  352.4 6.1 collective-permute-done
  362.9 5.2 collective-permute-done
  385.2 6.8 collective-permute-start
  392.1 5.6 collective-permute-done
  397.7 6.2 collective-permute-start
  404.0 4.5 collective-permute-done
  408.5 5.6 collective-permute-start
  418.0 6.5 collective-permute-start
  428.4 6.5 collective-permute-start
  438.9 6.5 collective-permute-start
  449.3 6.5 collective-permute-start
  459.7 6.5 collective-permute-start
  471.6 35.8 %while.34 = (s32[]{:T(128)}, f32[16,1,8,4096]{3,2,1,0:T(8,128)}, f32[16,1,8,16]{3,2,1,0:T(8,128)S(1)}, f32[16,1,8,4096]{3,2,1,0:T(8,128)}, f32[16,4096]{1,0:T(8,128)S(1)}, /*index=5*/f32[16,4096]{1,0:T(8,128)S(1)}, s32[]{:T(128)}) while((s32[]{:T(128)}, f32[16,1,8,4096]{3,2,1,0:T(8,128)}, f32[16,1,8,16]{3,2,1,0:T(8,128)S(1)}, ...), condition=%wide.region_16.17_spmd, body=%wide.region_14.16_spmd.sunk | while | flops 2064386 | bytes 1312853 | solution.py:65
  512.9 18.0 %all-to-all-start.2 = ((bf16[128,16,256]{2,0,1:T(8,128)(2,1)}), bf16[128,16,256]{2,0,1:T(8,128)(2,1)S(1)}, u32[]{:S(2)}, u32[]{:S(2)}) async-start(bf16[128,16,256]{2,0,1:T(8,128)(2,1)} %fusion.30), calls=%async_computation.2 | async-start | bytes 2097152 | tf_op jit(solution)/shard_map/all_to_all | solution.py:147
  532.1 12.2 %all-to-all-done.2 = bf16[128,16,256]{2,0,1:T(8,128)(2,1)S(1)} async-done(((bf16[128,16,256]{2,0,1:T(8,128)(2,1)}), bf16[128,16,256]{2,0,1:T(8,128)(2,1)S(1)}, u32[]{:S(2)}, u32[]{:S(2)}) %all-to-all-start.2) | async-done | bytes 1048608 | tf_op jit(solution)/shard_map/all_to_all | solution.py:147
  546.7 6.8 convolution_convert_fusion
  554.1 66.1 %all-reduce.6.cloned.1.call-done = bf16[16,4096]{1,0:T(8,128)(2,1)} async-done(((bf16[16,4096]{1,0:T(8,128)(2,1)}), bf16[16,4096]{1,0:T(8,128)(2,1)}) %all-reduce.6.cloned.1.call-update) | async-done | bytes 131088 | tf_op jit(solution)/shard_map/psum | solution.py:18
  620.9 13.0 %all-gather = f32[128,256]{1,0:T(8,128)S(1)} all-gather(f32[16,256]{1,0:T(8,128)S(1)} %dynamic-slice_convert_fusion), channel_id=2, replica_groups=mesh['req'=8,'seq'=16] {'req'}, dimensions={0}, use_global_device_ids=true | all-gather | bytes 147456 | tf_op jit(solution)/shard_map/all_gather | solution.py:157
  634.6 74.3 %reduce-scatter.2.cloned.1.call-done = bf16[128,2048]{1,0:T(8,128)(2,1)} async-done(((bf16[2048,2048]{1,0:T(8,128)(2,1)}), bf16[128,2048]{1,0:T(8,128)(2,1)}) %reduce-scatter.2.cloned.1.call-update) | async-done | bytes 524304 | tf_op jit(solution)/shard_map/reduce_scatter | solution.py:151
  (356 shorter events, 207.6 us)
Async XLA Ops:
  7.2 115.5 %copy-start = (bf16[256,160]{0,1:T(8,128)(2,1)S(1)}, bf16[256,160]{0,1:T(8,128)(2,1)}, u32[]{:S(2)}) copy-start(bf16[256,160]{0,1:T(8,128)(2,1)} %param.26) | copy-start | bytes 245764
  7.2 30.3 %all-gather.7.cloned.1.call-start = ((), (), s32[]{:S(2)}) async-start(), calls=%async_computation.5 | async-start | bytes 2359296 | tf_op jit(solution)/shard_map/all_gather | solution.py:95
  7.9 103.6 %all-gather.5.cloned.1.call-start = ((), (), s32[]{:S(2)}) async-start(), calls=%async_computation.4 | async-start | bytes 8912896 | tf_op jit(solution)/shard_map/all_gather | solution.py:98
  12.0 209.0 %all-reduce.4.cloned.1.call-start = ((), (), s32[]{:S(2)}) async-start(), calls=%async_computation.6 | async-start | bytes 2621440 | tf_op jit(solution)/shard_map/psum | solution.py:112
  125.5 5.5 copy-start.14
  125.5 95.4 %copy-start.11 = (bf16[128,256]{1,0:T(8,128)(2,1)S(1)}, bf16[128,256]{1,0:T(8,128)(2,1)}, u32[]{:S(2)}) copy-start(bf16[128,256]{1,0:T(8,128)(2,1)} %param.27) | copy-start | bytes 196612
  125.5 99.5 %all-to-all-start.1 = ((bf16[16,128,256]{2,1,0:T(8,128)(2,1)}), bf16[16,128,256]{2,1,0:T(8,128)(2,1)S(1)}, u32[]{:S(2)}, u32[]{:S(2)}) async-start(bf16[16,128,256]{2,1,0:T(8,128)(2,1)} %bitcast.17), calls=%async_computation.1 | async-start | bytes 2097152 | tf_op jit(solution)/shard_map/all_to_all | solution.py:123
  223.6 7.1 copy-start.9
  225.0 20.9 %all-to-all-start = ((bf16[16,128,256]{1,2,0:T(8,128)(2,1)}), bf16[16,128,256]{1,2,0:T(8,128)(2,1)S(1)}, u32[]{:S(2)}, u32[]{:S(2)}) async-start(bf16[16,128,256]{1,2,0:T(8,128)(2,1)} %copy.43), calls=%async_computation | async-start | bytes 2097152 | tf_op jit(solution)/shard_map/all_to_all | solution.py:124
  230.1 316.6 %all-gather.9.cloned.1.call-start = ((), (), s32[]{:S(2)}) async-start(), calls=%async_computation.7 | async-start | bytes 1179648 | tf_op jit(solution)/shard_map/all_gather | solution.py:122
  321.5 6.4 collective-permute-start
  328.0 9.4 %collective-permute-start = (f32[16,4096]{1,0:T(8,128)S(1)}, f32[16,4096]{1,0:T(8,128)S(1)}, u32[]{:S(2)}, u32[]{:S(2)}) collective-permute-start(f32[16,4096]{1,0:T(8,128)S(1)} %bitcast_add_fusion.3), channel_id=1, source_target_pairs={{0,1},{1,2},{2,3},{3,4},{4,5},{5,6},{6,7},{7,8},{8,9},{9,10},{10,1... | collective-permute-start | bytes 786440 | tf_op jit(solution)/shard_map/while/body/eval_jaxpr/ppermute | solution.py:13
  337.4 10.5 %collective-permute-start = (f32[16,4096]{1,0:T(8,128)S(1)}, f32[16,4096]{1,0:T(8,128)S(1)}, u32[]{:S(2)}, u32[]{:S(2)}) collective-permute-start(f32[16,4096]{1,0:T(8,128)S(1)} %bitcast_add_fusion.3), channel_id=1, source_target_pairs={{0,1},{1,2},{2,3},{3,4},{4,5},{5,6},{6,7},{7,8},{8,9},{9,10},{10,1... | collective-permute-start | bytes 786440 | tf_op jit(solution)/shard_map/while/body/eval_jaxpr/ppermute | solution.py:13
  347.9 10.5 %collective-permute-start = (f32[16,4096]{1,0:T(8,128)S(1)}, f32[16,4096]{1,0:T(8,128)S(1)}, u32[]{:S(2)}, u32[]{:S(2)}) collective-permute-start(f32[16,4096]{1,0:T(8,128)S(1)} %bitcast_add_fusion.3), channel_id=1, source_target_pairs={{0,1},{1,2},{2,3},{3,4},{4,5},{5,6},{6,7},{7,8},{8,9},{9,10},{10,1... | collective-permute-start | bytes 786440 | tf_op jit(solution)/shard_map/while/body/eval_jaxpr/ppermute | solution.py:13
  358.5 9.6 %collective-permute-start = (f32[16,4096]{1,0:T(8,128)S(1)}, f32[16,4096]{1,0:T(8,128)S(1)}, u32[]{:S(2)}, u32[]{:S(2)}) collective-permute-start(f32[16,4096]{1,0:T(8,128)S(1)} %bitcast_add_fusion.3), channel_id=1, source_target_pairs={{0,1},{1,2},{2,3},{3,4},{4,5},{5,6},{6,7},{7,8},{8,9},{9,10},{10,1... | collective-permute-start | bytes 786440 | tf_op jit(solution)/shard_map/while/body/eval_jaxpr/ppermute | solution.py:13
  368.1 8.8 %collective-permute-start = (f32[16,4096]{1,0:T(8,128)S(1)}, f32[16,4096]{1,0:T(8,128)S(1)}, u32[]{:S(2)}, u32[]{:S(2)}) collective-permute-start(f32[16,4096]{1,0:T(8,128)S(1)} %bitcast_add_fusion.3), channel_id=1, source_target_pairs={{0,1},{1,2},{2,3},{3,4},{4,5},{5,6},{6,7},{7,8},{8,9},{9,10},{10,1... | collective-permute-start | bytes 786440 | tf_op jit(solution)/shard_map/while/body/eval_jaxpr/ppermute | solution.py:13
  376.9 8.3 %collective-permute-start = (f32[16,4096]{1,0:T(8,128)S(1)}, f32[16,4096]{1,0:T(8,128)S(1)}, u32[]{:S(2)}, u32[]{:S(2)}) collective-permute-start(f32[16,4096]{1,0:T(8,128)S(1)} %bitcast_add_fusion.3), channel_id=1, source_target_pairs={{0,1},{1,2},{2,3},{3,4},{4,5},{5,6},{6,7},{7,8},{8,9},{9,10},{10,1... | collective-permute-start | bytes 786440 | tf_op jit(solution)/shard_map/while/body/eval_jaxpr/ppermute | solution.py:13
  385.2 12.5 %collective-permute-start = (f32[16,4096]{1,0:T(8,128)S(1)}, f32[16,4096]{1,0:T(8,128)S(1)}, u32[]{:S(2)}, u32[]{:S(2)}) collective-permute-start(f32[16,4096]{1,0:T(8,128)S(1)} %bitcast_add_fusion.3), channel_id=1, source_target_pairs={{0,1},{1,2},{2,3},{3,4},{4,5},{5,6},{6,7},{7,8},{8,9},{9,10},{10,1... | collective-permute-start | bytes 786440 | tf_op jit(solution)/shard_map/while/body/eval_jaxpr/ppermute | solution.py:13
  397.7 10.7 %collective-permute-start = (f32[16,4096]{1,0:T(8,128)S(1)}, f32[16,4096]{1,0:T(8,128)S(1)}, u32[]{:S(2)}, u32[]{:S(2)}) collective-permute-start(f32[16,4096]{1,0:T(8,128)S(1)} %bitcast_add_fusion.3), channel_id=1, source_target_pairs={{0,1},{1,2},{2,3},{3,4},{4,5},{5,6},{6,7},{7,8},{8,9},{9,10},{10,1... | collective-permute-start | bytes 786440 | tf_op jit(solution)/shard_map/while/body/eval_jaxpr/ppermute | solution.py:13
  408.5 9.5 %collective-permute-start = (f32[16,4096]{1,0:T(8,128)S(1)}, f32[16,4096]{1,0:T(8,128)S(1)}, u32[]{:S(2)}, u32[]{:S(2)}) collective-permute-start(f32[16,4096]{1,0:T(8,128)S(1)} %bitcast_add_fusion.3), channel_id=1, source_target_pairs={{0,1},{1,2},{2,3},{3,4},{4,5},{5,6},{6,7},{7,8},{8,9},{9,10},{10,1... | collective-permute-start | bytes 786440 | tf_op jit(solution)/shard_map/while/body/eval_jaxpr/ppermute | solution.py:13
  418.0 10.4 %collective-permute-start = (f32[16,4096]{1,0:T(8,128)S(1)}, f32[16,4096]{1,0:T(8,128)S(1)}, u32[]{:S(2)}, u32[]{:S(2)}) collective-permute-start(f32[16,4096]{1,0:T(8,128)S(1)} %bitcast_add_fusion.3), channel_id=1, source_target_pairs={{0,1},{1,2},{2,3},{3,4},{4,5},{5,6},{6,7},{7,8},{8,9},{9,10},{10,1... | collective-permute-start | bytes 786440 | tf_op jit(solution)/shard_map/while/body/eval_jaxpr/ppermute | solution.py:13
  428.4 10.4 %collective-permute-start = (f32[16,4096]{1,0:T(8,128)S(1)}, f32[16,4096]{1,0:T(8,128)S(1)}, u32[]{:S(2)}, u32[]{:S(2)}) collective-permute-start(f32[16,4096]{1,0:T(8,128)S(1)} %bitcast_add_fusion.3), channel_id=1, source_target_pairs={{0,1},{1,2},{2,3},{3,4},{4,5},{5,6},{6,7},{7,8},{8,9},{9,10},{10,1... | collective-permute-start | bytes 786440 | tf_op jit(solution)/shard_map/while/body/eval_jaxpr/ppermute | solution.py:13
  438.9 10.4 %collective-permute-start = (f32[16,4096]{1,0:T(8,128)S(1)}, f32[16,4096]{1,0:T(8,128)S(1)}, u32[]{:S(2)}, u32[]{:S(2)}) collective-permute-start(f32[16,4096]{1,0:T(8,128)S(1)} %bitcast_add_fusion.3), channel_id=1, source_target_pairs={{0,1},{1,2},{2,3},{3,4},{4,5},{5,6},{6,7},{7,8},{8,9},{9,10},{10,1... | collective-permute-start | bytes 786440 | tf_op jit(solution)/shard_map/while/body/eval_jaxpr/ppermute | solution.py:13
  449.3 10.4 %collective-permute-start = (f32[16,4096]{1,0:T(8,128)S(1)}, f32[16,4096]{1,0:T(8,128)S(1)}, u32[]{:S(2)}, u32[]{:S(2)}) collective-permute-start(f32[16,4096]{1,0:T(8,128)S(1)} %bitcast_add_fusion.3), channel_id=1, source_target_pairs={{0,1},{1,2},{2,3},{3,4},{4,5},{5,6},{6,7},{7,8},{8,9},{9,10},{10,1... | collective-permute-start | bytes 786440 | tf_op jit(solution)/shard_map/while/body/eval_jaxpr/ppermute | solution.py:13
  459.7 10.4 %collective-permute-start = (f32[16,4096]{1,0:T(8,128)S(1)}, f32[16,4096]{1,0:T(8,128)S(1)}, u32[]{:S(2)}, u32[]{:S(2)}) collective-permute-start(f32[16,4096]{1,0:T(8,128)S(1)} %bitcast_add_fusion.3), channel_id=1, source_target_pairs={{0,1},{1,2},{2,3},{3,4},{4,5},{5,6},{6,7},{7,8},{8,9},{9,10},{10,1... | collective-permute-start | bytes 786440 | tf_op jit(solution)/shard_map/while/body/eval_jaxpr/ppermute | solution.py:13
  512.9 18.1 %copy-start.5 = (f32[16,4096]{1,0:T(8,128)S(1)}, f32[16,4096]{1,0:T(8,128)}, u32[]{:S(2)}) copy-start(f32[16,4096]{1,0:T(8,128)} %param.29) | copy-start | bytes 786436
  512.9 18.1 %copy-start.7 = (f32[1,1,4096]{2,1,0:T(1,128)S(1)}, f32[1,1,4096]{2,1,0:T(1,128)}, u32[]{:S(2)}) copy-start(f32[1,1,4096]{2,1,0:T(1,128)} %copy-done.6) | copy-start | bytes 49156
  512.9 31.4 %all-to-all-start.2 = ((bf16[128,16,256]{2,0,1:T(8,128)(2,1)}), bf16[128,16,256]{2,0,1:T(8,128)(2,1)S(1)}, u32[]{:S(2)}, u32[]{:S(2)}) async-start(bf16[128,16,256]{2,0,1:T(8,128)(2,1)} %fusion.30), calls=%async_computation.2 | async-start | bytes 2097152 | tf_op jit(solution)/shard_map/all_to_all | solution.py:147
  531.0 89.2 %all-reduce.6.cloned.1.call-start = ((), (), s32[]{:S(2)}) async-start(), calls=%async_computation.9 | async-start | bytes 262144 | tf_op jit(solution)/shard_map/psum | solution.py:18
  531.8 177.1 %reduce-scatter.2.cloned.1.call-start = ((), (), s32[]{:S(2)}) async-start(), calls=%async_computation.8 | async-start | bytes 8912896 | tf_op jit(solution)/shard_map/reduce_scatter | solution.py:151
  553.5 155.5 %copy-start.2 = (bf16[1,128,2048]{2,1,0:T(8,128)(2,1)S(1)}, bf16[1,128,2048]{2,1,0:T(8,128)(2,1)}, u32[]{:S(2)}) copy-start(bf16[1,128,2048]{2,1,0:T(8,128)(2,1)} %param.19) | copy-start | bytes 1572868
  553.5 157.4 %copy-start.1 = (bf16[256,160]{0,1:T(8,128)(2,1)S(1)}, bf16[256,160]{0,1:T(8,128)(2,1)}, u32[]{:S(2)}) copy-start(bf16[256,160]{0,1:T(8,128)(2,1)} %param.26) | copy-start | bytes 245764
  (8 other events, 25.3 us)
Sparse Core Ops, SparseCore 0:
  9.7 27.7 all-gather.6
  40.2 71.2 all-gather.4
  125.6 95.2 all-reduce.3
  232.3 24.7 all-gather.8
  535.2 84.9 all-reduce.5
  623.5 85.3 reduce-scatter.1
where the time goes:
time: 720 us; the launch traced here: 718 us
  waiting for transfers between devices  415 us (58%)
  starting transfers between devices  109 us (15%)
  local copies, waits for them, and re-layouts  89.9 us (12%)
  other arithmetic  54.7 us (8%)
  matrix products  19.6 us (3%)
  between operations  14.4 us (2%)
  blocking collectives  13 us (2%)
    psum x1, waiting for transfers between devices, per_device(): summed = lax.psum(partial_proj, 'seq')  88.7 us
    ppermute x15, starting transfers between devices, shifted(): return lax.ppermute(block, axis, route)  80.1 us
    reduce_scatter x1, waiting for transfers between devices, per_device(): lax.psum_scatter(jnp.dot(gated_ch, w_out, preferred_element_type=jnp.floa...  74.3 us
    all_gather x1, waiting for transfers between devices, per_device(): lax.all_gather(normed, 'seq', axis=0, tiled=True)  72.3 us
    ppermute x15, waiting for transfers between devices, shifted(): return lax.ppermute(block, axis, route)  67.6 us
    psum x1, waiting for transfers between devices, spread(): return lax.psum(jnp.where(mine, array, jnp.zeros_like(array)), axis)  66.1 us
    squeeze x32, local copies, waits for them, and re-layouts, piece_scan(): lax.scan(advance, start, (to_blocks(rates), to_blocks(values), to_blocks(...  26.9 us
    all_gather x1, waiting for transfers between devices, per_device(): w_in = lax.all_gather(in_weight, 'req', axis=1, tiled=True)  25.4 us
  transfers between devices with their start and end apart: 24, of which 22 were waited for; matrix products, arithmetic and copies ran while one was open for 20% of the time, Pallas kernels for 0%

commit v1 on v0

--- a/solution.py
+++ b/solution.py
@@ -5,6 +5,9 @@
 
 STATE = 16
 RANK = 128
+layers_all_recast = lambda vector, axis_name: jnp.sum(
+    lax.all_gather(vector, axis_name=axis_name), axis=0
+)
 
 
 def shifted(block, axis, distance):
@@ -109,7 +112,7 @@
     inner = jax.nn.silu(convolved).astype(jnp.bfloat16)
     partial_proj = jnp.dot(inner, xproj_weight, preferred_element_type=jnp.float32)
     length_here = lax.dynamic_index_in_dim(lengths, req_index, 0, keepdims=False)
-    summed = lax.psum(partial_proj, "seq")
+    summed = layers_all_recast(partial_proj, "seq")
     live_all = (jnp.arange(span, dtype=jnp.int32) < length_here).astype(jnp.float32)
     rate_low = summed[:, :RANK].astype(jnp.bfloat16)
     delta_ch = (

time: 720 us -> 788 us (1.094)
  waiting for transfers between devices: 415 us -> 458 us
  local copies, waits for them, and re-layouts: 89.9 us -> 109 us
    all_gather x0 -> x1, waiting for transfers between devices: none -> 132 us  [lax.all_gather(vector, axis_name=axis_name)]
    psum x1 -> x0, waiting for transfers between devices: 88.7 us -> none  [per_device(): summed = lax.psum(partial_proj, 'seq')]
    unnamed x33 -> x36, local copies, waits for them, and re-layouts: 4.42 us -> 23.2 us
  transfers between devices with their start and end apart: 24 -> 24, of which waited for: 22 -> 22; matrix products, arithmetic and copies ran while one was open for 20% -> 22% of each run, Pallas kernels for 0% -> 0%
where the time goes in v1:
time: 788 us; the launch traced here: 786 us
  waiting for transfers between devices  458 us (58%)
  starting transfers between devices  111 us (14%)
  local copies, waits for them, and re-layouts  109 us (14%)
  other arithmetic  59.8 us (8%)
  matrix products  18.5 us (2%)
  between operations  14.5 us (2%)
  blocking collectives  13 us (2%)
    all_gather x1, waiting for transfers between devices, lax.all_gather(vector, axis_name=axis_name)  132 us
    ppermute x15, starting transfers between devices, shifted(): return lax.ppermute(block, axis, route)  82.2 us
    reduce_scatter x1, waiting for transfers between devices, per_device(): lax.psum_scatter(jnp.dot(gated_ch, w_out, preferred_element_type=jnp.floa...  74.3 us
    all_gather x1, waiting for transfers between devices, per_device(): lax.all_gather(normed, 'seq', axis=0, tiled=True)  72.3 us
    psum x1, waiting for transfers between devices, spread(): return lax.psum(jnp.where(mine, array, jnp.zeros_like(array)), axis)  66.2 us
    ppermute x15, waiting for transfers between devices, shifted(): return lax.ppermute(block, axis, route)  65.7 us
    squeeze x32, local copies, waits for them, and re-layouts, piece_scan(): lax.scan(advance, start, (to_blocks(rates), to_blocks(values), to_blocks(...  26.9 us
    all_gather x1, waiting for transfers between devices, per_device(): w_in = lax.all_gather(in_weight, 'req', axis=1, tiled=True)  25.4 us
  transfers between devices with their start and end apart: 24, of which 22 were waited for; matrix products, arithmetic and copies ran while one was open for 22% of the time, Pallas kernels for 0%

profile of v1, /device:TPU:0, one launch (start us, length us, event | category | flops | bytes accessed | tf_op | source)
XLA Modules:
  0.0 785.6 jit_solution(3152464345115488834)
XLA Ops:
  12.1 25.4 %all-gather.9.cloned.1.call-done = bf16[2,2048,256]{2,1,0:T(8,128)(2,1)} async-done(((bf16[2,256,256]{2,1,0:T(8,128)(2,1)}), bf16[2,2048,256]{2,1,0:T(8,128)(2,1)}) %all-gather.9.cloned.1.call-update) | async-done | bytes 2097168 | tf_op jit(solution)/shard_map/all_gather | solution.py:98
  39.2 72.3 %all-gather.7.cloned.1.call-done = bf16[2048,2048]{1,0:T(8,128)(2,1)} async-done(((bf16[128,2048]{1,0:T(8,128)(2,1)}), bf16[2048,2048]{1,0:T(8,128)(2,1)}) %all-gather.7.cloned.1.call-update) | async-done | bytes 8388624 | tf_op jit(solution)/shard_map/all_gather | solution.py:101
  111.5 6.9 fusion.33
  126.9 5.3 all-to-all-start.1
  132.2 131.8 %all-gather.13.cloned.1.call-done = f32[32768,160]{0,1:T(8,128)} async-done(((f32[2048,160]{0,1:T(8,128)}), f32[32768,160]{0,1:T(8,128)}) %all-gather.13.cloned.1.call-update) | async-done | bytes 20971536 | tf_op jit(solution)/shard_map/all_gather | solution.py:9
  264.0 18.8 %copy.61 = f32[20,8,16,2048]{3,2,1,0:T(8,128)S(1)} copy(f32[20,8,16,2048]{3,1,2,0:T(8,128)} %bitcast.317) | data formatting | bytes 41943040
  282.8 5.1 bitcast_reduce_fusion
  290.8 5.3 all-to-all-start
  304.4 9.2 %all-to-all-done = bf16[16,128,256]{1,2,0:T(8,128)(2,1)S(1)} async-done(((bf16[16,128,256]{1,2,0:T(8,128)(2,1)}), bf16[16,128,256]{1,2,0:T(8,128)(2,1)S(1)}, u32[]{:S(2)}, u32[]{:S(2)}) %all-to-all-start) | async-done | bytes 1048608 | tf_op jit(solution)/shard_map/all_to_all | solution.py:127
  323.4 65.9 %while.35 = (s32[]{:T(128)}, f32[1,16,4096]{2,1,0:T(8,128)S(1)}, f32[16,1,8,4096]{3,2,1,0:T(8,128)}, f32[16,1,8,4096]{3,2,1,0:T(8,128)}, f32[16,4096]{1,0:T(8,12...) while((s32[]{:T(128)}, f32[1,16,4096]{2,1,0:T(8,128)S(1)}, ...), condition=%wide.region_11.12_spmd.clone, body=%wide.region_2.11_spmd.clone.sunk | while | flops 4849667 | bytes 4347896 | solution.py:54
  389.3 148.8 %while.33 = (s32[]{:T(128)}, f32[16,4096]{1,0:T(8,128)S(1)}, f32[1,16,4096]{2,1,0:T(8,128)S(1)}, f32[1,16,4096]{2,1,0:T(8,128)S(1)}, s32[]{:T(128)}) while((s32[]{:T(128)}, f32[16,4096]{1,0:T(8,128)S(1)}, f32[1,16,4096]{2,1,0:T(8,128)S(1)}, f32[1,16,4096]{2,1,0:T(8,128)S(1)}, s32[]{:T(128)}) %tuple.127), condition=%wide.region_13.14_spmd, body=%wide.region_12.13_spmd.sunk | while | flops 131074 | bytes 2097253 | solution.py:143
  433.5 4.6 collective-permute-done
  438.2 6.0 collective-permute-start
  444.2 5.4 collective-permute-done
  449.6 7.2 collective-permute-start
  456.8 6.5 collective-permute-done
  463.4 7.1 collective-permute-start
  470.5 5.6 collective-permute-done
  476.2 6.2 collective-permute-start
  482.4 4.5 collective-permute-done
  486.9 5.6 collective-permute-start
  496.5 6.5 collective-permute-start
  506.9 6.5 collective-permute-start
  517.3 6.5 collective-permute-start
  527.7 6.5 collective-permute-start
  539.6 35.9 %while.34 = (s32[]{:T(128)}, f32[16,1,8,4096]{3,2,1,0:T(8,128)}, f32[16,1,8,16]{3,2,1,0:T(8,128)S(1)}, f32[16,1,8,4096]{3,2,1,0:T(8,128)}, f32[16,4096]{1,0:T(8,128)S(1)}, /*index=5*/f32[16,4096]{1,0:T(8,128)S(1)}, s32[]{:T(128)}) while((s32[]{:T(128)}, f32[16,1,8,4096]{3,2,1,0:T(8,128)}, f32[16,1,8,16]{3,2,1,0:T(8,128)S(1)}, ...), condition=%wide.region_16.17_spmd, body=%wide.region_14.16_spmd.sunk | while | flops 2064386 | bytes 1312853 | solution.py:68
  581.0 17.7 %all-to-all-start.2 = ((bf16[128,16,256]{2,0,1:T(8,128)(2,1)}), bf16[128,16,256]{2,0,1:T(8,128)(2,1)S(1)}, u32[]{:S(2)}, u32[]{:S(2)}) async-start(bf16[128,16,256]{2,0,1:T(8,128)(2,1)} %fusion.30), calls=%async_computation.2 | async-start | bytes 2097152 | tf_op jit(solution)/shard_map/all_to_all | solution.py:150
  599.8 12.2 %all-to-all-done.2 = bf16[128,16,256]{2,0,1:T(8,128)(2,1)S(1)} async-done(((bf16[128,16,256]{2,0,1:T(8,128)(2,1)}), bf16[128,16,256]{2,0,1:T(8,128)(2,1)S(1)}, u32[]{:S(2)}, u32[]{:S(2)}) %all-to-all-start.2) | async-done | bytes 1048608 | tf_op jit(solution)/shard_map/all_to_all | solution.py:150
  614.4 6.8 convolution_convert_fusion
  621.9 66.2 %all-reduce.3.cloned.1.call-done = bf16[16,4096]{1,0:T(8,128)(2,1)} async-done(((bf16[16,4096]{1,0:T(8,128)(2,1)}), bf16[16,4096]{1,0:T(8,128)(2,1)}) %all-reduce.3.cloned.1.call-update) | async-done | bytes 131088 | tf_op jit(solution)/shard_map/psum | solution.py:21
  688.8 13.0 %all-gather.1 = f32[128,256]{1,0:T(8,128)S(1)} all-gather(f32[16,256]{1,0:T(8,128)S(1)} %dynamic-slice_convert_fusion), channel_id=3, replica_groups=mesh['req'=8,'seq'=16] {'req'}, dimensions={0}, use_global_device_ids=true | all-gather | bytes 147456 | tf_op jit(solution)/shard_map/all_gather | solution.py:160
  702.5 74.3 %reduce-scatter.2.cloned.1.call-done = bf16[128,2048]{1,0:T(8,128)(2,1)} async-done(((bf16[2048,2048]{1,0:T(8,128)(2,1)}), bf16[128,2048]{1,0:T(8,128)(2,1)}) %reduce-scatter.2.cloned.1.call-update) | async-done | bytes 524304 | tf_op jit(solution)/shard_map/reduce_scatter | solution.py:154
  (360 shorter events, 214.4 us)
Async XLA Ops:
  7.2 115.5 %copy-start = (bf16[256,160]{0,1:T(8,128)(2,1)S(1)}, bf16[256,160]{0,1:T(8,128)(2,1)}, u32[]{:S(2)}) copy-start(bf16[256,160]{0,1:T(8,128)(2,1)} %param.26) | copy-start | bytes 245764
  7.2 30.3 %all-gather.9.cloned.1.call-start = ((), (), s32[]{:S(2)}) async-start(), calls=%async_computation.5 | async-start | bytes 2359296 | tf_op jit(solution)/shard_map/all_gather | solution.py:98
  7.9 103.6 %all-gather.7.cloned.1.call-start = ((), (), s32[]{:S(2)}) async-start(), calls=%async_computation.4 | async-start | bytes 8912896 | tf_op jit(solution)/shard_map/all_gather | solution.py:101
  12.0 252.1 %all-gather.13.cloned.1.call-start = ((), (), s32[]{:S(2)}) async-start(), calls=%async_computation.9 | async-start | bytes 22282240 | tf_op jit(solution)/shard_map/all_gather | solution.py:9
  126.9 163.9 %all-to-all-start.1 = ((bf16[16,128,256]{2,1,0:T(8,128)(2,1)}), bf16[16,128,256]{2,1,0:T(8,128)(2,1)S(1)}, u32[]{:S(2)}, u32[]{:S(2)}) async-start(bf16[16,128,256]{2,1,0:T(8,128)(2,1)} %bitcast.17), calls=%async_computation.1 | async-start | bytes 2097152 | tf_op jit(solution)/shard_map/all_to_all | solution.py:126
  282.8 5.1 copy-start.12
  289.5 7.2 copy-start.10
  290.8 22.8 %all-to-all-start = ((bf16[16,128,256]{1,2,0:T(8,128)(2,1)}), bf16[16,128,256]{1,2,0:T(8,128)(2,1)S(1)}, u32[]{:S(2)}, u32[]{:S(2)}) async-start(bf16[16,128,256]{1,2,0:T(8,128)(2,1)} %copy.50), calls=%async_computation | async-start | bytes 2097152 | tf_op jit(solution)/shard_map/all_to_all | solution.py:127
  296.1 318.3 %all-gather.11.cloned.1.call-start = ((), (), s32[]{:S(2)}) async-start(), calls=%async_computation.6 | async-start | bytes 1179648 | tf_op jit(solution)/shard_map/all_gather | solution.py:125
  315.4 5.4 copy-start.7
  389.4 6.0 collective-permute-start
  395.4 8.5 %collective-permute-start = (f32[16,4096]{1,0:T(8,128)S(1)}, f32[16,4096]{1,0:T(8,128)S(1)}, u32[]{:S(2)}, u32[]{:S(2)}) collective-permute-start(f32[16,4096]{1,0:T(8,128)S(1)} %bitcast_add_fusion.3), channel_id=1, source_target_pairs={{0,1},{1,2},{2,3},{3,4},{4,5},{5,6},{6,7},{7,8},{8,9},{9,10},{10,1... | collective-permute-start | bytes 786440 | tf_op jit(solution)/shard_map/while/body/eval_jaxpr/ppermute | solution.py:16
  404.0 8.3 %collective-permute-start = (f32[16,4096]{1,0:T(8,128)S(1)}, f32[16,4096]{1,0:T(8,128)S(1)}, u32[]{:S(2)}, u32[]{:S(2)}) collective-permute-start(f32[16,4096]{1,0:T(8,128)S(1)} %bitcast_add_fusion.3), channel_id=1, source_target_pairs={{0,1},{1,2},{2,3},{3,4},{4,5},{5,6},{6,7},{7,8},{8,9},{9,10},{10,1... | collective-permute-start | bytes 786440 | tf_op jit(solution)/shard_map/while/body/eval_jaxpr/ppermute | solution.py:16
  412.3 8.3 %collective-permute-start = (f32[16,4096]{1,0:T(8,128)S(1)}, f32[16,4096]{1,0:T(8,128)S(1)}, u32[]{:S(2)}, u32[]{:S(2)}) collective-permute-start(f32[16,4096]{1,0:T(8,128)S(1)} %bitcast_add_fusion.3), channel_id=1, source_target_pairs={{0,1},{1,2},{2,3},{3,4},{4,5},{5,6},{6,7},{7,8},{8,9},{9,10},{10,1... | collective-permute-start | bytes 786440 | tf_op jit(solution)/shard_map/while/body/eval_jaxpr/ppermute | solution.py:16
  420.6 8.4 %collective-permute-start = (f32[16,4096]{1,0:T(8,128)S(1)}, f32[16,4096]{1,0:T(8,128)S(1)}, u32[]{:S(2)}, u32[]{:S(2)}) collective-permute-start(f32[16,4096]{1,0:T(8,128)S(1)} %bitcast_add_fusion.3), channel_id=1, source_target_pairs={{0,1},{1,2},{2,3},{3,4},{4,5},{5,6},{6,7},{7,8},{8,9},{9,10},{10,1... | collective-permute-start | bytes 786440 | tf_op jit(solution)/shard_map/while/body/eval_jaxpr/ppermute | solution.py:16
  429.1 9.1 %collective-permute-start = (f32[16,4096]{1,0:T(8,128)S(1)}, f32[16,4096]{1,0:T(8,128)S(1)}, u32[]{:S(2)}, u32[]{:S(2)}) collective-permute-start(f32[16,4096]{1,0:T(8,128)S(1)} %bitcast_add_fusion.3), channel_id=1, source_target_pairs={{0,1},{1,2},{2,3},{3,4},{4,5},{5,6},{6,7},{7,8},{8,9},{9,10},{10,1... | collective-permute-start | bytes 786440 | tf_op jit(solution)/shard_map/while/body/eval_jaxpr/ppermute | solution.py:16
  438.2 11.4 %collective-permute-start = (f32[16,4096]{1,0:T(8,128)S(1)}, f32[16,4096]{1,0:T(8,128)S(1)}, u32[]{:S(2)}, u32[]{:S(2)}) collective-permute-start(f32[16,4096]{1,0:T(8,128)S(1)} %bitcast_add_fusion.3), channel_id=1, source_target_pairs={{0,1},{1,2},{2,3},{3,4},{4,5},{5,6},{6,7},{7,8},{8,9},{9,10},{10,1... | collective-permute-start | bytes 786440 | tf_op jit(solution)/shard_map/while/body/eval_jaxpr/ppermute | solution.py:16
  449.6 13.8 %collective-permute-start = (f32[16,4096]{1,0:T(8,128)S(1)}, f32[16,4096]{1,0:T(8,128)S(1)}, u32[]{:S(2)}, u32[]{:S(2)}) collective-permute-start(f32[16,4096]{1,0:T(8,128)S(1)} %bitcast_add_fusion.3), channel_id=1, source_target_pairs={{0,1},{1,2},{2,3},{3,4},{4,5},{5,6},{6,7},{7,8},{8,9},{9,10},{10,1... | collective-permute-start | bytes 786440 | tf_op jit(solution)/shard_map/while/body/eval_jaxpr/ppermute | solution.py:16
  463.4 12.7 %collective-permute-start = (f32[16,4096]{1,0:T(8,128)S(1)}, f32[16,4096]{1,0:T(8,128)S(1)}, u32[]{:S(2)}, u32[]{:S(2)}) collective-permute-start(f32[16,4096]{1,0:T(8,128)S(1)} %bitcast_add_fusion.3), channel_id=1, source_target_pairs={{0,1},{1,2},{2,3},{3,4},{4,5},{5,6},{6,7},{7,8},{8,9},{9,10},{10,1... | collective-permute-start | bytes 786440 | tf_op jit(solution)/shard_map/while/body/eval_jaxpr/ppermute | solution.py:16
  476.2 10.7 %collective-permute-start = (f32[16,4096]{1,0:T(8,128)S(1)}, f32[16,4096]{1,0:T(8,128)S(1)}, u32[]{:S(2)}, u32[]{:S(2)}) collective-permute-start(f32[16,4096]{1,0:T(8,128)S(1)} %bitcast_add_fusion.3), channel_id=1, source_target_pairs={{0,1},{1,2},{2,3},{3,4},{4,5},{5,6},{6,7},{7,8},{8,9},{9,10},{10,1... | collective-permute-start | bytes 786440 | tf_op jit(solution)/shard_map/while/body/eval_jaxpr/ppermute | solution.py:16
  486.9 9.5 %collective-permute-start = (f32[16,4096]{1,0:T(8,128)S(1)}, f32[16,4096]{1,0:T(8,128)S(1)}, u32[]{:S(2)}, u32[]{:S(2)}) collective-permute-start(f32[16,4096]{1,0:T(8,128)S(1)} %bitcast_add_fusion.3), channel_id=1, source_target_pairs={{0,1},{1,2},{2,3},{3,4},{4,5},{5,6},{6,7},{7,8},{8,9},{9,10},{10,1... | collective-permute-start | bytes 786440 | tf_op jit(solution)/shard_map/while/body/eval_jaxpr/ppermute | solution.py:16
  496.5 10.4 %collective-permute-start = (f32[16,4096]{1,0:T(8,128)S(1)}, f32[16,4096]{1,0:T(8,128)S(1)}, u32[]{:S(2)}, u32[]{:S(2)}) collective-permute-start(f32[16,4096]{1,0:T(8,128)S(1)} %bitcast_add_fusion.3), channel_id=1, source_target_pairs={{0,1},{1,2},{2,3},{3,4},{4,5},{5,6},{6,7},{7,8},{8,9},{9,10},{10,1... | collective-permute-start | bytes 786440 | tf_op jit(solution)/shard_map/while/body/eval_jaxpr/ppermute | solution.py:16
  506.9 10.4 %collective-permute-start = (f32[16,4096]{1,0:T(8,128)S(1)}, f32[16,4096]{1,0:T(8,128)S(1)}, u32[]{:S(2)}, u32[]{:S(2)}) collective-permute-start(f32[16,4096]{1,0:T(8,128)S(1)} %bitcast_add_fusion.3), channel_id=1, source_target_pairs={{0,1},{1,2},{2,3},{3,4},{4,5},{5,6},{6,7},{7,8},{8,9},{9,10},{10,1... | collective-permute-start | bytes 786440 | tf_op jit(solution)/shard_map/while/body/eval_jaxpr/ppermute | solution.py:16
  517.3 10.4 %collective-permute-start = (f32[16,4096]{1,0:T(8,128)S(1)}, f32[16,4096]{1,0:T(8,128)S(1)}, u32[]{:S(2)}, u32[]{:S(2)}) collective-permute-start(f32[16,4096]{1,0:T(8,128)S(1)} %bitcast_add_fusion.3), channel_id=1, source_target_pairs={{0,1},{1,2},{2,3},{3,4},{4,5},{5,6},{6,7},{7,8},{8,9},{9,10},{10,1... | collective-permute-start | bytes 786440 | tf_op jit(solution)/shard_map/while/body/eval_jaxpr/ppermute | solution.py:16
  527.7 10.4 %collective-permute-start = (f32[16,4096]{1,0:T(8,128)S(1)}, f32[16,4096]{1,0:T(8,128)S(1)}, u32[]{:S(2)}, u32[]{:S(2)}) collective-permute-start(f32[16,4096]{1,0:T(8,128)S(1)} %bitcast_add_fusion.3), channel_id=1, source_target_pairs={{0,1},{1,2},{2,3},{3,4},{4,5},{5,6},{6,7},{7,8},{8,9},{9,10},{10,1... | collective-permute-start | bytes 786440 | tf_op jit(solution)/shard_map/while/body/eval_jaxpr/ppermute | solution.py:16
  581.0 17.8 %copy-start.6 = (f32[16,4096]{1,0:T(8,128)S(1)}, f32[16,4096]{1,0:T(8,128)}, u32[]{:S(2)}) copy-start(f32[16,4096]{1,0:T(8,128)} %param.29) | copy-start | bytes 786436
  581.0 17.8 %copy-start.8 = (f32[1,1,4096]{2,1,0:T(1,128)S(1)}, f32[1,1,4096]{2,1,0:T(1,128)}, u32[]{:S(2)}) copy-start(f32[1,1,4096]{2,1,0:T(1,128)} %copy-done.7) | copy-start | bytes 49156
  581.0 31.0 %all-to-all-start.2 = ((bf16[128,16,256]{2,0,1:T(8,128)(2,1)}), bf16[128,16,256]{2,0,1:T(8,128)(2,1)S(1)}, u32[]{:S(2)}, u32[]{:S(2)}) async-start(bf16[128,16,256]{2,0,1:T(8,128)(2,1)} %fusion.30), calls=%async_computation.2 | async-start | bytes 2097152 | tf_op jit(solution)/shard_map/all_to_all | solution.py:150
  598.7 89.4 %all-reduce.3.cloned.1.call-start = ((), (), s32[]{:S(2)}) async-start(), calls=%async_computation.8 | async-start | bytes 262144 | tf_op jit(solution)/shard_map/psum | solution.py:21
  599.6 177.2 %reduce-scatter.2.cloned.1.call-start = ((), (), s32[]{:S(2)}) async-start(), calls=%async_computation.7 | async-start | bytes 8912896 | tf_op jit(solution)/shard_map/reduce_scatter | solution.py:154
  621.2 155.6 %copy-start.2 = (bf16[1,128,2048]{2,1,0:T(8,128)(2,1)S(1)}, bf16[1,128,2048]{2,1,0:T(8,128)(2,1)}, u32[]{:S(2)}) copy-start(bf16[1,128,2048]{2,1,0:T(8,128)(2,1)} %param.19) | copy-start | bytes 1572868
  621.3 157.5 %copy-start.1 = (bf16[256,160]{0,1:T(8,128)(2,1)S(1)}, bf16[256,160]{0,1:T(8,128)(2,1)}, u32[]{:S(2)}) copy-start(bf16[256,160]{0,1:T(8,128)(2,1)} %param.26) | copy-start | bytes 245764
  (9 other events, 21.7 us)
Sparse Core Ops, SparseCore 0:
  9.7 27.7 all-gather.8
  40.2 71.2 all-gather.6
  125.7 138.2 all-gather.12
  298.3 24.7 all-gather.10
  603.0 85.0 all-reduce.2
  691.4 85.3 reduce-scatter.1
